TPU v7x, 32 devices: a whole 2x2x4 slice. The times are simulated.
32 devices in a mesh: ckpt: 2 (over x), train: 4 (over z), tensor: 4 (over y, core).
Axes of the slice: x: 2, y: 2, z: 4, core: 2. Of those that a mesh axis runs over, the one named last changes fastest.
Arguments:
- hidden: bfloat16 [2, 2048, 28672], P('ckpt', 'train', 'tensor'), may hold values from -6 to 6
- out_grads: bfloat16 [2, 2048, 8192], P('ckpt', 'train', 'tensor'), may hold values from -6 to 6
- proj_in: bfloat16 [64, 28672], P(None, 'tensor'), may hold values from -0.03125 to 0.03125
- proj_out: bfloat16 [64, 8192], P(None, 'tensor'), may hold values from -0.0625 to 0.0625
- test_grads: bfloat16 [2, 64, 4096], P('ckpt', ('train', 'tensor')), may hold values from -6 to 6
- step_weights: int32 [2], P('ckpt'), may hold values from 1 to 4
Outputs:
- scores: float32 [16, 4, 16], P('train', None, 'tensor')
All inputs are finite; a program needn't handle non-finite values.
Results may differ from a plain program's by a relative error of at most 0.0029.
Values may be sent and summed in bfloat16 or wider, within the bound.
No kernel may reach another device: no remote copies, remote signals or barrier semaphores. Data moves between devices by JAX's collectives and lax.ppermute only.
A program may use at most 64 MiB of HBM per device.

v0:
```python
import math

import jax
import jax.numpy as jnp
from jax import lax
from jax.sharding import PartitionSpec as P

KIN = 64
KOUT = 64
SEQ = 128


def outer_grads(sides):
    blocks = sides.reshape(-1, SEQ, KIN + KOUT)
    left = blocks[:, :, :KIN]
    right = blocks[:, :, KIN:]
    outer = jnp.einsum("sto,sti->soi", right, left, precision=lax.Precision.HIGHEST)
    return outer.reshape(-1, KIN * KOUT).astype(jnp.bfloat16)


def body(hidden, out_grads, proj_in, proj_out, test_grads, step_weights):
    train_count = lax.axis_size("train")
    h_local = hidden[0]
    g_local = out_grads[0]
    contract = (((1,), (1,)), ((), ()))
    left = lax.dot_general(h_local, proj_in, contract, preferred_element_type=jnp.float32)
    right = lax.dot_general(g_local, proj_out, contract, preferred_element_type=jnp.float32)
    shared = lax.psum_scatter(
        jnp.concatenate([left, right], axis=1), "tensor", scatter_dimension=0, tiled=True
    )
    own = outer_grads(shared)
    train_block = lax.all_gather(own, "tensor", axis=0, tiled=True)
    tests = test_grads[0]
    width = tests.shape[0]
    examples = train_block.shape[0]
    table = lax.dot_general(
        train_block,
        lax.all_gather(test_grads, "train", axis=1, tiled=True)[0],
        contract,
        preferred_element_type=jnp.float32,
    )
    scale = 1.0 / math.sqrt(SEQ * KIN * KOUT)
    weight = step_weights[0].astype(jnp.float32) * scale
    total = lax.psum(table * weight, "ckpt")
    return total.reshape(examples, train_count, width)


def solution(mesh):
    placed = (
        P("ckpt", "train", "tensor"),
        P("ckpt", "train", "tensor"),
        P(None, "tensor"),
        P(None, "tensor"),
        P("ckpt", ("train", "tensor"), None),
        P("ckpt"),
    )
    return jax.shard_map(
        body, mesh=mesh, in_specs=placed, out_specs=P("train", None, "tensor"), check_vma=False
    )
```

profile of v0, /device:TPU:0, one launch (start us, length us, event | category | flops | bytes accessed | tf_op | source)
XLA Modules:
  0.0 55.8 jit_solution(17442658351243271955)
XLA Ops:
  6.5 0.0 copy-start
  6.5 0.0 copy-start.1
  6.5 0.0 copy-start.2
  6.5 0.0 reduce-scatter.2.cloned.1.call-start
  6.5 5.8 %fusion = f32[512,64]{0,1:T(8,128)S(1)} fusion(bf16[64,7168]{1,0:T(8,128)(2,1)} %param.8, bf16[1,512,7168]{2,1,0:T(8,128)(2,1)} %param.6), kind=kOutput, calls=%fused_computation | convolution fusion | flops 469762048 | bytes 8388608 | tf_op jit(solution)/shard_map/dot_general | solution.py:26
  12.3 0.0 copy-done
  12.3 0.0 copy-done.1
  12.3 0.8 %fusion.2 = f32[512,64]{0,1:T(8,128)S(1)} fusion(bf16[64,2048]{1,0:T(8,128)(2,1)S(1)} %copy-done.1, bf16[1,512,2048]{2,1,0:T(8,128)(2,1)S(1)} %copy-done), kind=kOutput, calls=%fused_computation.2 | convolution fusion | flops 134217728 | bytes 2490368 | tf_op jit(solution)/shard_map/dot_general | solution.py:27
  13.1 0.7 %pad_maximum_fusion = f32[512,128]{0,1:T(8,128)} fusion(f32[512,64]{0,1:T(8,128)S(1)} %fusion.2, f32[512,64]{0,1:T(8,128)S(1)} %fusion), kind=kLoop, calls=%fused_computation.6 | loop fusion | flops 65536 | bytes 524288 | tf_op jit(solution)/shard_map/concatenate | solution.py:29
  13.8 0.0 reduce-scatter.2.cloned.1.call-update
  13.8 0.0 copy-done.2
  13.8 0.1 copy.9
  14.5 15.6 %all_gather.7 = bf16[1,16,4096]{2,0,1:T(2,128)(2,1)S(1)} all-gather(bf16[1,4,4096]{2,0,1:T(2,128)(2,1)S(1)} %copy.9), channel_id=1, replica_groups=mesh['ckpt'=2,'train'=4,'tensor'=4] {'train'}, dimensions={1}, use_global_device_ids=true | all-gather | bytes 163840 | tf_op jit(solution)/shard_map/all_gather | solution.py:38
  30.2 6.5 %reduce-scatter.2.cloned.1.call-done = f32[128,128]{0,1:T(8,128)} async-done(((f32[512,128]{0,1:T(8,128)}), f32[128,128]{0,1:T(8,128)}) %reduce-scatter.2.cloned.1.call-update) | async-done | bytes 65552 | tf_op jit(solution)/shard_map/reduce_scatter | solution.py:28
  36.7 1.0 %convolution_convert_fusion = bf16[64,64]{1,0:T(8,128)(2,1)S(1)} fusion(f32[1,128,128]{1,2,0:T(8,128)} %bitcast.22), kind=kOutput, calls=%fused_computation.4 | convolution fusion | flops 6295552 | bytes 73728 | tf_op jit(solution)/shard_map/sto,sti->soi/dot_general | solution.py:17
  37.7 0.1 reshape.35
  37.8 5.2 %all-gather = bf16[4,1,4096]{2,1,0:T(2,128)(2,1)S(1)} all-gather(bf16[1,1,4096]{2,1,0:T(2,128)(2,1)S(1)} %reshape.35), channel_id=1, replica_groups=mesh['ckpt'=2,'train'=4,'tensor'=4] {'tensor'}, dimensions={0}, use_global_device_ids=true | all-gather | bytes 40960 | tf_op jit(solution)/shard_map/all_gather | solution.py:32
  43.0 0.3 convolution_multiply_fusion
  43.3 0.1 reshape.34
  43.4 5.6 %psum.7 = f32[4,4,4]{2,1,0:T(4,128)} all-reduce(f32[4,4,4]{2,1,0:T(4,128)S(1)} %reshape.34), channel_id=1, replica_groups=mesh['ckpt'=2,'train'=4,'tensor'=4] {'ckpt'}, use_global_device_ids=true, to_apply=%region_1.0 | all-reduce | flops 64 | bytes 512 | tf_op jit(solution)/shard_map/psum | solution.py:44
Async XLA Ops:
  6.5 5.8 %copy-start = (bf16[1,512,2048]{2,1,0:T(8,128)(2,1)S(1)}, bf16[1,512,2048]{2,1,0:T(8,128)(2,1)}, u32[]{:S(2)}) copy-start(bf16[1,512,2048]{2,1,0:T(8,128)(2,1)} %param.7) | copy-start | bytes 6291460
  6.5 5.8 %copy-start.1 = (bf16[64,2048]{1,0:T(8,128)(2,1)S(1)}, bf16[64,2048]{1,0:T(8,128)(2,1)}, u32[]{:S(2)}) copy-start(bf16[64,2048]{1,0:T(8,128)(2,1)} %param.9) | copy-start | bytes 786436
  6.5 7.3 %copy-start.2 = (bf16[1,4,4096]{2,1,0:T(4,128)(2,1)S(1)}, bf16[1,4,4096]{2,1,0:T(4,128)(2,1)}, u32[]{:S(2)}) copy-start(bf16[1,4,4096]{2,1,0:T(4,128)(2,1)} %param.10) | copy-start | bytes 98308
  6.5 30.2 %reduce-scatter.2.cloned.1.call-start = ((), (), s32[]{:S(2)}) async-start(), calls=%async_computation.1 | async-start | bytes 327680 | tf_op jit(solution)/shard_map/reduce_scatter | solution.py:28
Sparse Core Ops, SparseCore 0:
  13.9 22.7 reduce-scatter.1
where the time goes:
time: 56 us; the launch traced here: 55.8 us
  blocking collectives  26.4 us (47%)
  between operations  14.1 us (25%)
  matrix products  7.76 us (14%)
  waiting for transfers between devices  6.55 us (12%)
  other arithmetic  0.72 us (1%)
    all_gather x1, blocking collectives, body(): lax.all_gather(test_grads, 'train', axis=1, tiled=True)[0]  15.6 us
    reduce_scatter x1, waiting for transfers between devices, body(): lax.psum_scatter(jnp.concatenate([left, right], axis=1), 'tensor', scatte...  6.54 us
    dot_general x1, matrix products, body(): lax.dot_general(h_local, proj_in, contract, preferred_element_type=jnp.fl...  5.76 us
    psum x1, blocking collectives, body(): total = lax.psum(table * weight, 'ckpt')  5.56 us
    all_gather x1, blocking collectives, body(): train_block = lax.all_gather(own, 'tensor', axis=0, tiled=True)  5.23 us
  transfers between devices with their start and end apart: 1, of which 1 were waited for; matrix products, arithmetic and copies ran while one was open for 0% of the time, Pallas kernels for 0%

commit v1 on v0

v1 whole, which is shorter than its diff:
```python
import math

import jax
import jax.numpy as jnp
from jax import lax
from jax.sharding import PartitionSpec as P

KIN = 64
KOUT = 64
SEQ = 128


def outer_grads(sides):
    blocks = sides.reshape(-1, SEQ, KIN + KOUT)
    left = blocks[:, :, :KIN]
    right = blocks[:, :, KIN:]
    outer = jnp.einsum("sto,sti->soi", right, left, precision=lax.Precision.HIGHEST)
    return outer.reshape(-1, KIN * KOUT).astype(jnp.bfloat16)


def from_shift(x, axis, n, s):
    return lax.ppermute(x, axis, [((i + s) % n, i) for i in range(n)])


def gather(x, axis):
    n = lax.axis_size(axis)
    me = lax.axis_index(axis)
    pieces = jnp.stack([x] + [from_shift(x, axis, n, s) for s in range(1, n)])
    twice = jnp.concatenate([pieces, pieces])
    return lax.dynamic_slice_in_dim(twice, (n - me) % n, n, axis=0)


def reduce_scatter(x, axis):
    n = lax.axis_size(axis)
    me = lax.axis_index(axis)
    total = lax.dynamic_index_in_dim(x, me, axis=0, keepdims=False)
    for s in range(1, n):
        block = lax.dynamic_index_in_dim(x, (me + n - s) % n, axis=0, keepdims=False)
        total = total + from_shift(block, axis, n, s)
    return total


def body(hidden, out_grads, proj_in, proj_out, test_grads, step_weights):
    n_tensor = lax.axis_size("tensor")
    n_train = lax.axis_size("train")
    tests = gather(test_grads[0], "train")
    tests = tests.reshape(-1, tests.shape[-1])
    contract = (((1,), (1,)), ((), ()))
    left = lax.dot_general(hidden[0], proj_in, contract, preferred_element_type=jnp.float32)
    right = lax.dot_general(out_grads[0], proj_out, contract, preferred_element_type=jnp.float32)
    sides = jnp.concatenate([left, right], axis=1)
    sides = sides.reshape(n_tensor, -1, sides.shape[-1])
    own = outer_grads(reduce_scatter(sides, "tensor"))
    train_block = gather(own, "tensor").reshape(-1, own.shape[-1])
    table = lax.dot_general(train_block, tests, contract, preferred_element_type=jnp.float32)
    scale = 1.0 / math.sqrt(SEQ * KIN * KOUT)
    weight = step_weights[0].astype(jnp.float32) * scale
    terms = gather(table * weight, "ckpt")
    total = terms[0]
    for c in range(1, terms.shape[0]):
        total = total + terms[c]
    return total.reshape(train_block.shape[0], n_train, -1)


def solution(mesh):
    placed = (
        P("ckpt", "train", "tensor"),
        P("ckpt", "train", "tensor"),
        P(None, "tensor"),
        P(None, "tensor"),
        P("ckpt", ("train", "tensor"), None),
        P("ckpt"),
    )
    return jax.shard_map(
        body, mesh=mesh, in_specs=placed, out_specs=P("train", None, "tensor"), check_vma=False
    )
```

time: 56 us -> 30.2 us (0.54)
  blocking collectives: 26.4 us -> 0 us
  between operations: 14.1 us -> 0.83 us
  starting transfers between devices: 0.01 us -> 12.9 us
  local copies, waits for them, and re-layouts: 0.24 us -> 1.65 us
  other arithmetic: 0.72 us -> 0.05 us
    all_gather x2 -> x0, blocking collectives: 20.9 us -> none  [the longest x1 15.6 us: body(): lax.all_gather(test_grads, 'train', axis=1, tiled=True)[0]]
    ppermute x0 -> x10, starting transfers between devices: none -> 12.9 us  [from_shift(): return lax.ppermute(x, axis, [((i + s) % n, i) for i in range(n)])]
    ppermute x0 -> x10, waiting for transfers between devices: none -> 6.95 us  [from_shift(): return lax.ppermute(x, axis, [((i + s) % n, i) for i in range(n)])]
    reduce_scatter x1 -> x0, waiting for transfers between devices: 6.54 us -> none  [body(): lax.psum_scatter(jnp.concatenate([left, right], axis=1), 'tensor', scatte...]
    psum x1 -> x0, blocking collectives: 5.56 us -> none  [body(): total = lax.psum(table * weight, 'ckpt')]
    dot_general x1, matrix products: 0.95 us -> 0.18 us  [outer_grads(): jnp.einsum('sto,sti->soi', right, left, precision=lax.Precision.HIGHEST)]
    add x0 -> x1, local copies, waits for them, and re-layouts: none -> 0.68 us  [body(): total = total + terms[c]]
    concatenate x1 -> x2, other arithmetic: 0.72 us -> 0.04 us  [the longest x1 0.02 us: body(): sides = jnp.concatenate([left, right], axis=1)]
  transfers between devices with their start and end apart: 1 -> 10, of which waited for: 1 -> 5; matrix products, arithmetic and copies ran while one was open for 0% -> 27% of each run, Pallas kernels for 0% -> 0%
where the time goes in v1:
time: 30.2 us; the launch traced here: 30.1 us
  starting transfers between devices  12.9 us (43%)
  matrix products  7.65 us (25%)
  waiting for transfers between devices  6.95 us (23%)
  local copies, waits for them, and re-layouts  1.65 us (5%)
  between operations  0.83 us (3%)
    ppermute x10, starting transfers between devices, from_shift(): return lax.ppermute(x, axis, [((i + s) % n, i) for i in range(n)])  12.9 us
    ppermute x10, waiting for transfers between devices, from_shift(): return lax.ppermute(x, axis, [((i + s) % n, i) for i in range(n)])  6.95 us
    dot_general x1, matrix products, body(): lax.dot_general(hidden[0], proj_in, contract, preferred_element_type=jnp....  5.61 us
    dot_general x1, matrix products, body(): lax.dot_general(out_grads[0], proj_out, contract, preferred_element_type=...  1.7 us
    add x1, local copies, waits for them, and re-layouts, body(): total = total + terms[c]  0.68 us
  transfers between devices with their start and end apart: 10, of which 5 were waited for; matrix products, arithmetic and copies ran while one was open for 27% of the time, Pallas kernels for 0%

profile of v1, /device:TPU:0, one launch (start us, length us, event | category | flops | bytes accessed | tf_op | source)
XLA Modules:
  0.0 30.1 jit_solution(15195785672553120733)
XLA Ops:
  0.0 5.0 %collective-permute-start.6 = (bf16[4,4096]{1,0:T(4,128)(2,1)}, bf16[4,4096]{1,0:T(4,128)(2,1)S(1)}, u32[]{:S(2)}, u32[]{:S(2)}) collective-permute-start(bf16[4,4096]{1,0:T(4,128)(2,1)} %bitcast.47), channel_id=1, source_target_pairs={{4,0},{8,4},{12,8},{0,12},{5,1},{9,5},{13,9},{1,13},{6,2},{10,6},{... | collective-permute-start | bytes 98312 | tf_op jit(solution)/shard_map/ppermute | solution.py:22
  5.1 1.0 %collective-permute-start.8 = (bf16[4,4096]{1,0:T(4,128)(2,1)}, bf16[4,4096]{1,0:T(4,128)(2,1)S(1)}, u32[]{:S(2)}, u32[]{:S(2)}) collective-permute-start(bf16[4,4096]{1,0:T(4,128)(2,1)} %bitcast.49), channel_id=1, source_target_pairs={{12,0},{0,4},{4,8},{8,12},{13,1},{1,5},{5,9},{9,13},{14,2},{2,6},{... | collective-permute-start | bytes 98312 | tf_op jit(solution)/shard_map/ppermute | solution.py:22
  6.1 1.7 %fusion.2 = f32[512,64]{0,1:T(8,128)S(1)} fusion(bf16[64,2048]{1,0:T(8,128)(2,1)} %param.9, bf16[1,512,2048]{2,1,0:T(8,128)(2,1)S(1)} %copy-done), kind=kOutput, calls=%fused_computation.2 | convolution fusion | flops 134217728 | bytes 2490368 | tf_op jit(solution)/shard_map/dot_general | solution.py:50
  7.8 5.6 %fusion = f32[512,64]{0,1:T(8,128)S(1)} fusion(bf16[64,7168]{1,0:T(8,128)(2,1)} %param.8, bf16[1,512,7168]{2,1,0:T(8,128)(2,1)} %param.6), kind=kOutput, calls=%fused_computation | convolution fusion | flops 469762048 | bytes 8388608 | tf_op jit(solution)/shard_map/dot_general | solution.py:49
  13.4 0.1 reshape.52
  13.5 0.2 constant_dynamic-slice_fusion.3
  13.8 0.1 collective-permute-start.2
  13.8 1.6 %collective-permute-start.1 = (f32[128,128]{0,1:T(8,128)S(1)}, f32[128,128]{0,1:T(8,128)S(1)}, u32[]{:S(2)}, u32[]{:S(2)}) collective-permute-start(f32[128,128]{0,1:T(8,128)S(1)} %bitcast.57), channel_id=1, source_target_pairs={{2,0},{3,1},{0,2},{1,3},{6,4},{7,5},{4,6},{5,7},{10,8},{11,9},{8,1... | collective-permute-start | bytes 196616 | tf_op jit(solution)/shard_map/ppermute | solution.py:22
  16.1 1.4 %collective-permute-start = (f32[128,128]{0,1:T(8,128)S(1)}, f32[128,128]{0,1:T(8,128)S(1)}, u32[]{:S(2)}, u32[]{:S(2)}) collective-permute-start(f32[128,128]{0,1:T(8,128)S(1)} %bitcast.56), channel_id=1, source_target_pairs={{1,0},{2,1},{3,2},{0,3},{5,4},{6,5},{7,6},{4,7},{9,8},{10,9},{11,1... | collective-permute-start | bytes 196616 | tf_op jit(solution)/shard_map/ppermute | solution.py:22
  17.6 0.0 collective-permute-done.7
  17.8 0.6 %collective-permute-done.1 = f32[128,128]{0,1:T(8,128)S(1)} collective-permute-done((f32[128,128]{0,1:T(8,128)S(1)}, f32[128,128]{0,1:T(8,128)S(1)}, u32[]{:S(2)}, u32[]{:S(2)}) %collective-permute-start.1) | collective-permute-done | bytes 65568 | tf_op jit(solution)/shard_map/ppermute | solution.py:22
  18.4 1.1 %collective-permute-done = f32[128,128]{0,1:T(8,128)S(1)} collective-permute-done((f32[128,128]{0,1:T(8,128)S(1)}, f32[128,128]{0,1:T(8,128)S(1)}, u32[]{:S(2)}, u32[]{:S(2)}) %collective-permute-start) | collective-permute-done | bytes 65568 | tf_op jit(solution)/shard_map/ppermute | solution.py:22
  19.5 0.2 convolution_convert_fusion
  19.7 0.1 convert_element_type.30
  19.8 1.8 %collective-permute-start.3 = (bf16[1,4096]{1,0:T(2,128)(2,1)S(1)}, bf16[1,4096]{1,0:T(2,128)(2,1)S(1)}, u32[]{:S(2)}, u32[]{:S(2)}) collective-permute-start(bf16[1,4096]{1,0:T(2,128)(2,1)S(1)} %convert_element_type.30), channel_id=1, source_target_pairs={{1,0},{2,1},{3,2},{0,3},{5,4},{6,5},{7,6},{4,7},{9,8},{10,9},{11,1... | collective-permute-start | bytes 24584 | tf_op jit(solution)/shard_map/ppermute | solution.py:22
  21.6 0.5 %collective-permute-start.4 = (bf16[1,4096]{1,0:T(2,128)(2,1)S(1)}, bf16[1,4096]{1,0:T(2,128)(2,1)S(1)}, u32[]{:S(2)}, u32[]{:S(2)}) collective-permute-start(bf16[1,4096]{1,0:T(2,128)(2,1)S(1)} %convert_element_type.30), channel_id=1, source_target_pairs={{2,0},{3,1},{0,2},{1,3},{6,4},{7,5},{4,6},{5,7},{10,8},{11,9},{8,1... | collective-permute-start | bytes 24584 | tf_op jit(solution)/shard_map/ppermute | solution.py:22
  22.2 0.1 convert_element_type.29
  22.3 0.8 %collective-permute-done.3 = bf16[1,4096]{1,0:T(2,128)(2,1)S(1)} collective-permute-done((bf16[1,4096]{1,0:T(2,128)(2,1)S(1)}, bf16[1,4096]{1,0:T(2,128)(2,1)S(1)}, u32[]{:S(2)}, u32[]{:S(2)}) %collective-permute-start.3) | collective-permute-done | bytes 8224 | tf_op jit(solution)/shard_map/ppermute | solution.py:22
  23.0 2.4 %collective-permute-done.4 = bf16[1,4096]{1,0:T(2,128)(2,1)S(1)} collective-permute-done((bf16[1,4096]{1,0:T(2,128)(2,1)S(1)}, bf16[1,4096]{1,0:T(2,128)(2,1)S(1)}, u32[]{:S(2)}, u32[]{:S(2)}) %collective-permute-start.4) | collective-permute-done | bytes 8224 | tf_op jit(solution)/shard_map/ppermute | solution.py:22
  25.4 0.2 concatenate.16
  25.6 0.2 convolution_multiply_fusion
  25.8 1.5 %collective-permute-start.9 = (f32[4,16]{1,0:T(4,128)S(1)}, f32[4,16]{1,0:T(4,128)S(1)}, u32[]{:S(2)}, u32[]{:S(2)}) collective-permute-start(f32[4,16]{1,0:T(4,128)S(1)} %convolution_multiply_fusion), channel_id=1, source_target_pairs={{16,0},{0,16},{17,1},{1,17},{18,2},{2,18},{19,3},{3,19},{20,4},{4,... | collective-permute-start | bytes 776 | tf_op jit(solution)/shard_map/ppermute | solution.py:22
  27.3 2.1 %collective-permute-done.9 = f32[4,16]{1,0:T(4,128)S(1)} collective-permute-done((f32[4,16]{1,0:T(4,128)S(1)}, f32[4,16]{1,0:T(4,128)S(1)}, u32[]{:S(2)}, u32[]{:S(2)}) %collective-permute-start.9) | collective-permute-done | bytes 288 | tf_op jit(solution)/shard_map/ppermute | solution.py:22
  29.4 0.7 %add.86 = f32[4,4,4]{2,1,0:T(4,128)} reshape(f32[1,4,16]{2,1,0:T(4,128)S(1)} %slice_add_fusion) | data formatting | bytes 512 | tf_op jit(solution)/shard_map/add | solution.py:61
  (24 shorter events, 0.3 us)
Async XLA Ops:
  0.0 6.1 %copy-start = (bf16[1,512,2048]{2,1,0:T(8,128)(2,1)S(1)}, bf16[1,512,2048]{2,1,0:T(8,128)(2,1)}, u32[]{:S(2)}) copy-start(bf16[1,512,2048]{2,1,0:T(8,128)(2,1)} %param.7) | copy-start | bytes 6291460
  0.0 15.4 %copy-start.1 = (bf16[1,4,4096]{2,1,0:T(4,128)(2,1)S(1)}, bf16[1,4,4096]{2,1,0:T(4,128)(2,1)}, u32[]{:S(2)}) copy-start(bf16[1,4,4096]{2,1,0:T(4,128)(2,1)} %param.10) | copy-start | bytes 98308
  0.0 16.1 %collective-permute-start.6 = (bf16[4,4096]{1,0:T(4,128)(2,1)}, bf16[4,4096]{1,0:T(4,128)(2,1)S(1)}, u32[]{:S(2)}, u32[]{:S(2)}) collective-permute-start(bf16[4,4096]{1,0:T(4,128)(2,1)} %bitcast.47), channel_id=1, source_target_pairs={{4,0},{8,4},{12,8},{0,12},{5,1},{9,5},{13,9},{1,13},{6,2},{10,6},{... | collective-permute-start | bytes 98312 | tf_op jit(solution)/shard_map/ppermute | solution.py:22
  5.1 12.6 %collective-permute-start.7 = (bf16[4,4096]{1,0:T(4,128)(2,1)}, bf16[4,4096]{1,0:T(4,128)(2,1)S(1)}, u32[]{:S(2)}, u32[]{:S(2)}) collective-permute-start(bf16[4,4096]{1,0:T(4,128)(2,1)} %bitcast.48), channel_id=1, source_target_pairs={{8,0},{12,4},{0,8},{4,12},{9,1},{13,5},{1,9},{5,13},{10,2},{14,6},... | collective-permute-start | bytes 98312 | tf_op jit(solution)/shard_map/ppermute | solution.py:22
  5.1 12.6 %collective-permute-start.8 = (bf16[4,4096]{1,0:T(4,128)(2,1)}, bf16[4,4096]{1,0:T(4,128)(2,1)S(1)}, u32[]{:S(2)}, u32[]{:S(2)}) collective-permute-start(bf16[4,4096]{1,0:T(4,128)(2,1)} %bitcast.49), channel_id=1, source_target_pairs={{12,0},{0,4},{4,8},{8,12},{13,1},{1,5},{5,9},{9,13},{14,2},{2,6},{... | collective-permute-start | bytes 98312 | tf_op jit(solution)/shard_map/ppermute | solution.py:22
  13.8 4.0 %collective-permute-start.2 = (f32[128,128]{0,1:T(8,128)S(1)}, f32[128,128]{0,1:T(8,128)S(1)}, u32[]{:S(2)}, u32[]{:S(2)}) collective-permute-start(f32[128,128]{0,1:T(8,128)S(1)} %bitcast.58), channel_id=1, source_target_pairs={{3,0},{0,1},{1,2},{2,3},{7,4},{4,5},{5,6},{6,7},{11,8},{8,9},{9,10... | collective-permute-start | bytes 196616 | tf_op jit(solution)/shard_map/ppermute | solution.py:22
  13.8 4.6 %collective-permute-start.1 = (f32[128,128]{0,1:T(8,128)S(1)}, f32[128,128]{0,1:T(8,128)S(1)}, u32[]{:S(2)}, u32[]{:S(2)}) collective-permute-start(f32[128,128]{0,1:T(8,128)S(1)} %bitcast.57), channel_id=1, source_target_pairs={{2,0},{3,1},{0,2},{1,3},{6,4},{7,5},{4,6},{5,7},{10,8},{11,9},{8,1... | collective-permute-start | bytes 196616 | tf_op jit(solution)/shard_map/ppermute | solution.py:22
  16.1 3.3 %collective-permute-start = (f32[128,128]{0,1:T(8,128)S(1)}, f32[128,128]{0,1:T(8,128)S(1)}, u32[]{:S(2)}, u32[]{:S(2)}) collective-permute-start(f32[128,128]{0,1:T(8,128)S(1)} %bitcast.56), channel_id=1, source_target_pairs={{1,0},{2,1},{3,2},{0,3},{5,4},{6,5},{7,6},{4,7},{9,8},{10,9},{11,1... | collective-permute-start | bytes 196616 | tf_op jit(solution)/shard_map/ppermute | solution.py:22
  19.8 3.2 %collective-permute-start.3 = (bf16[1,4096]{1,0:T(2,128)(2,1)S(1)}, bf16[1,4096]{1,0:T(2,128)(2,1)S(1)}, u32[]{:S(2)}, u32[]{:S(2)}) collective-permute-start(bf16[1,4096]{1,0:T(2,128)(2,1)S(1)} %convert_element_type.30), channel_id=1, source_target_pairs={{1,0},{2,1},{3,2},{0,3},{5,4},{6,5},{7,6},{4,7},{9,8},{10,9},{11,1... | collective-permute-start | bytes 24584 | tf_op jit(solution)/shard_map/ppermute | solution.py:22
  21.6 3.8 %collective-permute-start.4 = (bf16[1,4096]{1,0:T(2,128)(2,1)S(1)}, bf16[1,4096]{1,0:T(2,128)(2,1)S(1)}, u32[]{:S(2)}, u32[]{:S(2)}) collective-permute-start(bf16[1,4096]{1,0:T(2,128)(2,1)S(1)} %convert_element_type.30), channel_id=1, source_target_pairs={{2,0},{3,1},{0,2},{1,3},{6,4},{7,5},{4,6},{5,7},{10,8},{11,9},{8,1... | collective-permute-start | bytes 24584 | tf_op jit(solution)/shard_map/ppermute | solution.py:22
  22.1 3.3 %collective-permute-start.5 = (bf16[1,4096]{1,0:T(2,128)(2,1)S(1)}, bf16[1,4096]{1,0:T(2,128)(2,1)S(1)}, u32[]{:S(2)}, u32[]{:S(2)}) collective-permute-start(bf16[1,4096]{1,0:T(2,128)(2,1)S(1)} %convert_element_type.30), channel_id=1, source_target_pairs={{3,0},{0,1},{1,2},{2,3},{7,4},{4,5},{5,6},{6,7},{11,8},{8,9},{9,10... | collective-permute-start | bytes 24584 | tf_op jit(solution)/shard_map/ppermute | solution.py:22
  25.8 3.6 %collective-permute-start.9 = (f32[4,16]{1,0:T(4,128)S(1)}, f32[4,16]{1,0:T(4,128)S(1)}, u32[]{:S(2)}, u32[]{:S(2)}) collective-permute-start(f32[4,16]{1,0:T(4,128)S(1)} %convolution_multiply_fusion), channel_id=1, source_target_pairs={{16,0},{0,16},{17,1},{1,17},{18,2},{2,18},{19,3},{3,19},{20,4},{4,... | collective-permute-start | bytes 776 | tf_op jit(solution)/shard_map/ppermute | solution.py:22

commit v2 on v1

v2 whole, which is shorter than its diff:
```python
import math

import jax
import jax.numpy as jnp
from jax import lax
from jax.sharding import PartitionSpec as P

KIN = 64
KOUT = 64
SEQ = 128


def outer_grads(sides):
    blocks = sides.reshape(-1, SEQ, KIN + KOUT)
    left = blocks[:, :, :KIN]
    right = blocks[:, :, KIN:]
    outer = jnp.einsum("sto,sti->soi", right, left, precision=lax.Precision.HIGHEST)
    return outer.reshape(-1, KIN * KOUT).astype(jnp.bfloat16)


def swap(x, axis, mask):
    n = lax.axis_size(axis)
    return lax.ppermute(x, axis, [(i, i ^ mask) for i in range(n)])


def high(axis, mask):
    return (lax.axis_index(axis) & mask) != 0


def masks_of(axis, start=0):
    n = lax.axis_size(axis)
    return [1 << b for b in range(start, n.bit_length() - 1)]


def gather(x, axis, masks):
    for mask in masks:
        other = swap(x, axis, mask)
        x = jnp.where(high(axis, mask), jnp.concatenate([other, x]), jnp.concatenate([x, other]))
    return x


def body(hidden, out_grads, proj_in, proj_out, test_grads, step_weights):
    n_train = lax.axis_size("train")
    tests = gather(test_grads[0], "train", masks_of("train"))
    contract = (((1,), (1,)), ((), ()))
    left = lax.dot_general(hidden[0], proj_in, contract, preferred_element_type=jnp.float32)
    right = lax.dot_general(out_grads[0], proj_out, contract, preferred_element_type=jnp.float32)
    sides = jnp.concatenate([left, right], axis=1)
    halves = sides.reshape(2, -1, sides.shape[-1])
    upper = high("tensor", 1)
    kept = jnp.where(upper, halves[1], halves[0])
    sent = jnp.where(upper, halves[0], halves[1])
    part = kept + swap(sent, "tensor", 1)
    for mask in masks_of("tensor", 1):
        part = part + swap(part, "tensor", mask)
    own = outer_grads(part)
    train_block = gather(own, "tensor", [1])
    table = lax.dot_general(train_block, tests, contract, preferred_element_type=jnp.float32)
    scale = 1.0 / math.sqrt(SEQ * KIN * KOUT)
    total = table * (step_weights[0].astype(jnp.float32) * scale)
    for mask in masks_of("ckpt"):
        total = total + swap(total, "ckpt", mask)
    return total.reshape(train_block.shape[0], n_train, -1)


def solution(mesh):
    placed = (
        P("ckpt", "train", "tensor"),
        P("ckpt", "train", "tensor"),
        P(None, "tensor"),
        P(None, "tensor"),
        P("ckpt", ("train", "tensor"), None),
        P("ckpt"),
    )
    return jax.shard_map(
        body, mesh=mesh, in_specs=placed, out_specs=P("train", None, "tensor"), check_vma=False
    )
```

time: 30.2 us -> 22 us (0.73)
  starting transfers between devices: 12.9 us -> 9.34 us
  waiting for transfers between devices: 6.95 us -> 3.88 us
  local copies, waits for them, and re-layouts: 1.65 us -> 0.88 us
  matrix products: 7.65 us -> 6.95 us
    ppermute x10 -> x6, starting transfers between devices: 12.9 us -> 9.34 us  [swap(): return lax.ppermute(x, axis, [(i, i ^ mask) for i in range(n)])]
    ppermute x10 -> x6, waiting for transfers between devices: 6.95 us -> 3.88 us  [swap(): return lax.ppermute(x, axis, [(i, i ^ mask) for i in range(n)])]
    dot_general x1, matrix products: 1.7 us -> 0.76 us  [body(): lax.dot_general(out_grads[0], proj_out, contract, preferred_element_type=...]
    add x1 -> x0, local copies, waits for them, and re-layouts: 0.68 us -> none  [body(): total = total + terms[c]]
    reshape x2, local copies, waits for them, and re-layouts: 0.13 us -> 0.75 us  [the longest x1 0.68 us: body(): return total.reshape(train_block.shape[0], n_train, -1)]
  transfers between devices with their start and end apart: 10 -> 6, of which waited for: 5 -> 4; matrix products, arithmetic and copies ran while one was open for 27% -> 2% of each run, Pallas kernels for 0% -> 0%
where the time goes in v2:
time: 22 us; the launch traced here: 21.9 us
  starting transfers between devices  9.34 us (42%)
  matrix products  6.95 us (32%)
  waiting for transfers between devices  3.88 us (18%)
  local copies, waits for them, and re-layouts  0.88 us (4%)
  between operations  0.73 us (3%)
    ppermute x6, starting transfers between devices, swap(): return lax.ppermute(x, axis, [(i, i ^ mask) for i in range(n)])  9.34 us
    dot_general x1, matrix products, body(): lax.dot_general(hidden[0], proj_in, contract, preferred_element_type=jnp....  5.76 us
    ppermute x6, waiting for transfers between devices, swap(): return lax.ppermute(x, axis, [(i, i ^ mask) for i in range(n)])  3.88 us
    dot_general x1, matrix products, body(): lax.dot_general(out_grads[0], proj_out, contract, preferred_element_type=...  0.76 us
    reshape x1, local copies, waits for them, and re-layouts, body(): return total.reshape(train_block.shape[0], n_train, -1)  0.68 us
  transfers between devices with their start and end apart: 6, of which 4 were waited for; matrix products, arithmetic and copies ran while one was open for 2% of the time, Pallas kernels for 0%

profile of v2, /device:TPU:0, one launch (start us, length us, event | category | flops | bytes accessed | tf_op | source)
XLA Modules:
  0.0 21.9 jit_solution(13485669504931310503)
XLA Ops:
  0.0 0.0 copy-start
  0.0 5.8 %fusion = f32[512,64]{0,1:T(8,128)S(1)} fusion(bf16[64,7168]{1,0:T(8,128)(2,1)} %param.8, bf16[1,512,7168]{2,1,0:T(8,128)(2,1)} %param.6), kind=kOutput, calls=%fused_computation | convolution fusion | flops 469762048 | bytes 8388608 | tf_op jit(solution)/shard_map/dot_general | solution.py:46
  5.8 0.0 copy-done
  5.8 0.0 copy-done.1
  5.8 0.8 %fusion.2 = f32[512,64]{0,1:T(8,128)S(1)} fusion(bf16[64,2048]{1,0:T(8,128)(2,1)S(1)} %copy-done.1, bf16[1,512,2048]{2,1,0:T(8,128)(2,1)S(1)} %copy-done), kind=kOutput, calls=%fused_computation.2 | convolution fusion | flops 134217728 | bytes 2490368 | tf_op jit(solution)/shard_map/dot_general | solution.py:47
  6.6 0.5 %collective-permute-start = (f32[256,128]{0,1:T(8,128)S(1)}, f32[256,128]{0,1:T(8,128)S(1)}, u32[]{:S(2)}, u32[]{:S(2)}) collective-permute-start(f32[256,128]{0,1:T(8,128)S(1)} %broadcast_select_fusion), channel_id=1, source_target_pairs={{0,1},{1,0},{2,3},{3,2},{4,5},{5,4},{6,7},{7,6},{8,9},{9,8},{10,11... | collective-permute-start | bytes 393224 | tf_op jit(solution)/shard_map/ppermute | solution.py:23
  7.1 0.0 copy-done.2
  7.1 2.7 %collective-permute-start.3 = (bf16[4,4096]{1,0:T(4,128)(2,1)S(1)}, bf16[4,4096]{1,0:T(4,128)(2,1)S(1)}, u32[]{:S(2)}, u32[]{:S(2)}) collective-permute-start(bf16[4,4096]{1,0:T(4,128)(2,1)S(1)} %bitcast.12), channel_id=1, source_target_pairs={{0,4},{4,0},{8,12},{12,8},{1,5},{5,1},{9,13},{13,9},{2,6},{6,2},{1... | collective-permute-start | bytes 98312 | tf_op jit(solution)/shard_map/ppermute | solution.py:23
  9.8 0.0 collective-permute-done
  9.8 1.6 %collective-permute-start.1 = (f32[256,128]{0,1:T(8,128)S(1)}, f32[256,128]{0,1:T(8,128)S(1)}, u32[]{:S(2)}, u32[]{:S(2)}) collective-permute-start(f32[256,128]{0,1:T(8,128)S(1)} %select_add_fusion), channel_id=1, source_target_pairs={{0,2},{1,3},{2,0},{3,1},{4,6},{5,7},{6,4},{7,5},{8,10},{9,11},{10,... | collective-permute-start | bytes 393224 | tf_op jit(solution)/shard_map/ppermute | solution.py:23
  11.4 0.4 %collective-permute-done.3 = bf16[4,4096]{1,0:T(4,128)(2,1)S(1)} collective-permute-done((bf16[4,4096]{1,0:T(4,128)(2,1)S(1)}, bf16[4,4096]{1,0:T(4,128)(2,1)S(1)}, u32[]{:S(2)}, u32[]{:S(2)}) %collective-permute-start.3) | collective-permute-done | bytes 32800 | tf_op jit(solution)/shard_map/ppermute | solution.py:23
  11.7 0.1 maximum_select_fusion.2
  11.8 3.0 %collective-permute-start.4 = (bf16[8,4096]{1,0:T(8,128)(2,1)S(1)}, bf16[8,4096]{1,0:T(8,128)(2,1)S(1)}, u32[]{:S(2)}, u32[]{:S(2)}) collective-permute-start(bf16[8,4096]{1,0:T(8,128)(2,1)S(1)} %maximum_select_fusion.2), channel_id=1, source_target_pairs={{0,8},{4,12},{8,0},{12,4},{1,9},{5,13},{9,1},{13,5},{2,10},{6,14},... | collective-permute-start | bytes 196616 | tf_op jit(solution)/shard_map/ppermute | solution.py:23
  14.8 0.6 %collective-permute-done.1 = f32[256,128]{0,1:T(8,128)S(1)} collective-permute-done((f32[256,128]{0,1:T(8,128)S(1)}, f32[256,128]{0,1:T(8,128)S(1)}, u32[]{:S(2)}, u32[]{:S(2)}) %collective-permute-start.1) | collective-permute-done | bytes 131104 | tf_op jit(solution)/shard_map/ppermute | solution.py:23
  15.4 0.1 reshape.16
  15.5 0.2 %convolution_convert_fusion = bf16[2,64,64]{2,1,0:T(8,128)(2,1)S(1)} fusion(f32[2,128,64]{1,0,2:T(2,128)S(1)} %get-tuple-element.6, f32[2,128,64]{1,0,2:T(2,128)S(1)} %get-tuple-element.5), kind=kOutput, calls=%fused_computation.4 | convolution fusion | flops 12591104 | bytes 147456 | tf_op jit(solution)/shard_map/sto,sti->soi/dot_general | solution.py:17
  15.8 0.1 convert_element_type.11
  15.9 0.1 collective-permute-start.2
  16.6 0.8 %collective-permute-done.4 = bf16[8,4096]{1,0:T(8,128)(2,1)S(1)} collective-permute-done((bf16[8,4096]{1,0:T(8,128)(2,1)S(1)}, bf16[8,4096]{1,0:T(8,128)(2,1)S(1)}, u32[]{:S(2)}, u32[]{:S(2)}) %collective-permute-start.4) | collective-permute-done | bytes 65568 | tf_op jit(solution)/shard_map/ppermute | solution.py:23
  17.4 0.0 collective-permute-done.2
  17.4 0.2 convolution_multiply_fusion
  17.6 1.5 %collective-permute-start.5 = (f32[4,16]{1,0:T(4,128)S(1)}, f32[4,16]{1,0:T(4,128)S(1)}, u32[]{:S(2)}, u32[]{:S(2)}) collective-permute-start(f32[4,16]{1,0:T(4,128)S(1)} %convolution_multiply_fusion), channel_id=1, source_target_pairs={{0,16},{16,0},{1,17},{17,1},{2,18},{18,2},{3,19},{19,3},{4,20},{20... | collective-permute-start | bytes 776 | tf_op jit(solution)/shard_map/ppermute | solution.py:23
  19.1 2.1 %collective-permute-done.5 = f32[4,16]{1,0:T(4,128)S(1)} collective-permute-done((f32[4,16]{1,0:T(4,128)S(1)}, f32[4,16]{1,0:T(4,128)S(1)}, u32[]{:S(2)}, u32[]{:S(2)}) %collective-permute-start.5) | collective-permute-done | bytes 288 | tf_op jit(solution)/shard_map/ppermute | solution.py:23
  21.2 0.7 %reshape.17 = f32[4,4,4]{2,1,0:T(4,128)} reshape(f32[4,16]{1,0:T(4,128)S(1)} %add.11) | data formatting | bytes 512 | tf_op jit(solution)/shard_map/reshape | solution.py:63
  (7 shorter events, 0.1 us)
Async XLA Ops:
  0.0 5.8 %copy-start = (bf16[1,512,2048]{2,1,0:T(8,128)(2,1)S(1)}, bf16[1,512,2048]{2,1,0:T(8,128)(2,1)}, u32[]{:S(2)}) copy-start(bf16[1,512,2048]{2,1,0:T(8,128)(2,1)} %param.7) | copy-start | bytes 6291460
  0.0 5.8 %copy-start.1 = (bf16[64,2048]{1,0:T(8,128)(2,1)S(1)}, bf16[64,2048]{1,0:T(8,128)(2,1)}, u32[]{:S(2)}) copy-start(bf16[64,2048]{1,0:T(8,128)(2,1)} %param.9) | copy-start | bytes 786436
  0.0 7.1 %copy-start.2 = (bf16[1,4,4096]{2,1,0:T(4,128)(2,1)S(1)}, bf16[1,4,4096]{2,1,0:T(4,128)(2,1)}, u32[]{:S(2)}) copy-start(bf16[1,4,4096]{2,1,0:T(4,128)(2,1)} %param.10) | copy-start | bytes 98308
  6.6 3.2 %collective-permute-start = (f32[256,128]{0,1:T(8,128)S(1)}, f32[256,128]{0,1:T(8,128)S(1)}, u32[]{:S(2)}, u32[]{:S(2)}) collective-permute-start(f32[256,128]{0,1:T(8,128)S(1)} %broadcast_select_fusion), channel_id=1, source_target_pairs={{0,1},{1,0},{2,3},{3,2},{4,5},{5,4},{6,7},{7,6},{8,9},{9,8},{10,11... | collective-permute-start | bytes 393224 | tf_op jit(solution)/shard_map/ppermute | solution.py:23
  7.1 4.6 %collective-permute-start.3 = (bf16[4,4096]{1,0:T(4,128)(2,1)S(1)}, bf16[4,4096]{1,0:T(4,128)(2,1)S(1)}, u32[]{:S(2)}, u32[]{:S(2)}) collective-permute-start(bf16[4,4096]{1,0:T(4,128)(2,1)S(1)} %bitcast.12), channel_id=1, source_target_pairs={{0,4},{4,0},{8,12},{12,8},{1,5},{5,1},{9,13},{13,9},{2,6},{6,2},{1... | collective-permute-start | bytes 98312 | tf_op jit(solution)/shard_map/ppermute | solution.py:23
  9.8 5.6 %collective-permute-start.1 = (f32[256,128]{0,1:T(8,128)S(1)}, f32[256,128]{0,1:T(8,128)S(1)}, u32[]{:S(2)}, u32[]{:S(2)}) collective-permute-start(f32[256,128]{0,1:T(8,128)S(1)} %select_add_fusion), channel_id=1, source_target_pairs={{0,2},{1,3},{2,0},{3,1},{4,6},{5,7},{6,4},{7,5},{8,10},{9,11},{10,... | collective-permute-start | bytes 393224 | tf_op jit(solution)/shard_map/ppermute | solution.py:23
  11.8 5.6 %collective-permute-start.4 = (bf16[8,4096]{1,0:T(8,128)(2,1)S(1)}, bf16[8,4096]{1,0:T(8,128)(2,1)S(1)}, u32[]{:S(2)}, u32[]{:S(2)}) collective-permute-start(bf16[8,4096]{1,0:T(8,128)(2,1)S(1)} %maximum_select_fusion.2), channel_id=1, source_target_pairs={{0,8},{4,12},{8,0},{12,4},{1,9},{5,13},{9,1},{13,5},{2,10},{6,14},... | collective-permute-start | bytes 196616 | tf_op jit(solution)/shard_map/ppermute | solution.py:23
  15.9 1.6 %collective-permute-start.2 = (bf16[2,4096]{1,0:T(2,128)(2,1)S(1)}, bf16[2,4096]{1,0:T(2,128)(2,1)S(1)}, u32[]{:S(2)}, u32[]{:S(2)}) collective-permute-start(bf16[2,4096]{1,0:T(2,128)(2,1)S(1)} %convert_element_type.11), channel_id=1, source_target_pairs={{0,1},{1,0},{2,3},{3,2},{4,5},{5,4},{6,7},{7,6},{8,9},{9,8},{10,11... | collective-permute-start | bytes 49160 | tf_op jit(solution)/shard_map/ppermute | solution.py:23
  17.6 3.6 %collective-permute-start.5 = (f32[4,16]{1,0:T(4,128)S(1)}, f32[4,16]{1,0:T(4,128)S(1)}, u32[]{:S(2)}, u32[]{:S(2)}) collective-permute-start(f32[4,16]{1,0:T(4,128)S(1)} %convolution_multiply_fusion), channel_id=1, source_target_pairs={{0,16},{16,0},{1,17},{17,1},{2,18},{18,2},{3,19},{19,3},{4,20},{20... | collective-permute-start | bytes 776 | tf_op jit(solution)/shard_map/ppermute | solution.py:23

commit v3 on v2

--- a/solution.py
+++ b/solution.py
@@ -3,6 +3,8 @@
 import jax
 import jax.numpy as jnp
 from jax import lax
+from jax.experimental import pallas as pl
+from jax.experimental.pallas import tpu as pltpu
 from jax.sharding import PartitionSpec as P
 
 KIN = 64
@@ -16,6 +18,50 @@
     right = blocks[:, :, KIN:]
     outer = jnp.einsum("sto,sti->soi", right, left, precision=lax.Precision.HIGHEST)
     return outer.reshape(-1, KIN * KOUT).astype(jnp.bfloat16)
+
+
+def project_kernel(upper_ref, lower_ref, proj_ref, out_ref, acc):
+    step = pl.program_id(0)
+
+    @pl.when(step == 0)
+    def _():
+        acc[...] = jnp.zeros_like(acc)
+
+    rows = upper_ref.shape[0]
+    contract = (((1,), (1,)), ((), ()))
+    for j, ref in enumerate((upper_ref, lower_ref)):
+        acc[:, j * rows:(j + 1) * rows] += lax.dot_general(
+            proj_ref[...], ref[...], contract, preferred_element_type=jnp.float32
+        )
+
+    @pl.when(step == pl.num_programs(0) - 1)
+    def _():
+        out_ref[...] = acc[...]
+
+
+def project_t(x, proj):
+    rows, depth = x.shape
+    width = proj.shape[0]
+    chunk = depth // 2 if depth % 256 == 0 else depth
+    half = rows // 2
+    return pl.pallas_call(
+        project_kernel,
+        out_shape=jax.ShapeDtypeStruct((width, rows), jnp.float32),
+        grid=(depth // chunk,),
+        in_specs=[
+            pl.BlockSpec((half, chunk), lambda k: (0, k)),
+            pl.BlockSpec((half, chunk), lambda k: (1, k)),
+            pl.BlockSpec((width, chunk), lambda k: (0, k)),
+        ],
+        out_specs=pl.BlockSpec((width, rows), lambda k: (0, 0)),
+        scratch_shapes=[pltpu.VMEM((width, rows), jnp.float32)],
+        compiler_params=pltpu.CompilerParams(dimension_semantics=("arbitrary",)),
+        cost_estimate=pl.CostEstimate(
+            flops=2 * rows * depth * width,
+            bytes_accessed=2 * rows * depth + 2 * width * depth + 4 * width * rows,
+            transcendentals=0,
+        ),
+    )(x, x, proj)
 
 
 def swap(x, axis, mask):
@@ -43,7 +89,7 @@
     n_train = lax.axis_size("train")
     tests = gather(test_grads[0], "train", masks_of("train"))
     contract = (((1,), (1,)), ((), ()))
-    left = lax.dot_general(hidden[0], proj_in, contract, preferred_element_type=jnp.float32)
+    left = project_t(hidden[0], proj_in).T
     right = lax.dot_general(out_grads[0], proj_out, contract, preferred_element_type=jnp.float32)
     sides = jnp.concatenate([left, right], axis=1)
     halves = sides.reshape(2, -1, sides.shape[-1])

time: 22 us -> 21.8 us (level)
  matrix products: 6.95 us -> 1.19 us
  Pallas kernels: 0 us -> 5.39 us
    dot_general x1 -> x0, matrix products: 5.76 us -> none  [body(): lax.dot_general(hidden[0], proj_in, contract, preferred_element_type=jnp....]
    pallas_call x0 -> x1, Pallas kernels: none -> 5.39 us  [project_t(): pl.pallas_call(project_kernel, out_shape=jax.ShapeDtypeStruct((width, row...]
where the time goes in v3:
time: 21.8 us; the launch traced here: 21.7 us
  starting transfers between devices  9.35 us (43%)
  Pallas kernels  5.39 us (25%)
  waiting for transfers between devices  3.88 us (18%)
  matrix products  1.19 us (5%)
  local copies, waits for them, and re-layouts  1.01 us (5%)
  between operations  0.72 us (3%)
    ppermute x6, starting transfers between devices, swap(): return lax.ppermute(x, axis, [(i, i ^ mask) for i in range(n)])  9.35 us
    pallas_call x1, Pallas kernels, project_t(): pl.pallas_call(project_kernel, out_shape=jax.ShapeDtypeStruct((width, row...  5.39 us
    ppermute x6, waiting for transfers between devices, swap(): return lax.ppermute(x, axis, [(i, i ^ mask) for i in range(n)])  3.88 us
    dot_general x1, matrix products, body(): lax.dot_general(out_grads[0], proj_out, contract, preferred_element_type=...  0.76 us
    reshape x1, local copies, waits for them, and re-layouts, body(): return total.reshape(train_block.shape[0], n_train, -1)  0.68 us
  transfers between devices with their start and end apart: 6, of which 4 were waited for; matrix products, arithmetic and copies ran while one was open for 2% of the time, Pallas kernels for 0%

profile of v3, /device:TPU:0, one launch (start us, length us, event | category | flops | bytes accessed | tf_op | source)
XLA Modules:
  0.0 21.7 jit_solution(4244972105886952219)
XLA Ops:
  0.0 0.0 copy-start
  0.0 5.4 %shard_map.64 = f32[64,512]{1,0:T(8,128)} custom-call(bf16[512,7168]{1,0:T(8,128)(2,1)} %bitcast.10, bf16[512,7168]{1,0:T(8,128)(2,1)} %bitcast.11, bf16[64,7168]{1,0:T(8,128)(2,1)} %proj_ref.1), custom_call_target="tpu_custom_call" | custom-call | flops 469762048 | bytes 8388608 | tf_op jit(solution)/shard_map/pallas_call | solution.py:47
  5.4 0.0 copy-done.2
  5.4 0.0 copy-start.3
  5.4 0.8 %fusion = f32[512,64]{0,1:T(8,128)S(1)} fusion(bf16[64,2048]{1,0:T(8,128)(2,1)S(1)} %copy-done.2, bf16[1,512,2048]{2,1,0:T(8,128)(2,1)S(1)} %copy-done), kind=kOutput, calls=%fused_computation | convolution fusion | flops 134217728 | bytes 2490368 | tf_op jit(solution)/shard_map/dot_general | solution.py:93
  6.2 0.1 copy-done.1
  6.3 0.5 %collective-permute-start = (f32[256,128]{0,1:T(8,128)S(1)}, f32[256,128]{0,1:T(8,128)S(1)}, u32[]{:S(2)}, u32[]{:S(2)}) collective-permute-start(f32[256,128]{0,1:T(8,128)S(1)} %broadcast_select_fusion), channel_id=1, source_target_pairs={{0,1},{1,0},{2,3},{3,2},{4,5},{5,4},{6,7},{7,6},{8,9},{9,8},{10,11... | collective-permute-start | bytes 393224 | tf_op jit(solution)/shard_map/ppermute | solution.py:69
  6.9 2.7 %collective-permute-start.3 = (bf16[4,4096]{1,0:T(4,128)(2,1)S(1)}, bf16[4,4096]{1,0:T(4,128)(2,1)S(1)}, u32[]{:S(2)}, u32[]{:S(2)}) collective-permute-start(bf16[4,4096]{1,0:T(4,128)(2,1)S(1)} %bitcast.14), channel_id=1, source_target_pairs={{0,4},{4,0},{8,12},{12,8},{1,5},{5,1},{9,13},{13,9},{2,6},{6,2},{1... | collective-permute-start | bytes 98312 | tf_op jit(solution)/shard_map/ppermute | solution.py:69
  9.5 0.0 collective-permute-done
  9.5 1.6 %collective-permute-start.1 = (f32[256,128]{0,1:T(8,128)S(1)}, f32[256,128]{0,1:T(8,128)S(1)}, u32[]{:S(2)}, u32[]{:S(2)}) collective-permute-start(f32[256,128]{0,1:T(8,128)S(1)} %select_add_fusion), channel_id=1, source_target_pairs={{0,2},{1,3},{2,0},{3,1},{4,6},{5,7},{6,4},{7,5},{8,10},{9,11},{10,... | collective-permute-start | bytes 393224 | tf_op jit(solution)/shard_map/ppermute | solution.py:69
  11.1 0.4 %collective-permute-done.3 = bf16[4,4096]{1,0:T(4,128)(2,1)S(1)} collective-permute-done((bf16[4,4096]{1,0:T(4,128)(2,1)S(1)}, bf16[4,4096]{1,0:T(4,128)(2,1)S(1)}, u32[]{:S(2)}, u32[]{:S(2)}) %collective-permute-start.3) | collective-permute-done | bytes 32800 | tf_op jit(solution)/shard_map/ppermute | solution.py:69
  11.5 0.1 maximum_select_fusion.2
  11.6 3.0 %collective-permute-start.4 = (bf16[8,4096]{1,0:T(8,128)(2,1)S(1)}, bf16[8,4096]{1,0:T(8,128)(2,1)S(1)}, u32[]{:S(2)}, u32[]{:S(2)}) collective-permute-start(bf16[8,4096]{1,0:T(8,128)(2,1)S(1)} %maximum_select_fusion.2), channel_id=1, source_target_pairs={{0,8},{4,12},{8,0},{12,4},{1,9},{5,13},{9,1},{13,5},{2,10},{6,14},... | collective-permute-start | bytes 196616 | tf_op jit(solution)/shard_map/ppermute | solution.py:69
  14.6 0.6 %collective-permute-done.1 = f32[256,128]{0,1:T(8,128)S(1)} collective-permute-done((f32[256,128]{0,1:T(8,128)S(1)}, f32[256,128]{0,1:T(8,128)S(1)}, u32[]{:S(2)}, u32[]{:S(2)}) %collective-permute-start.1) | collective-permute-done | bytes 131104 | tf_op jit(solution)/shard_map/ppermute | solution.py:69
  15.2 0.1 reshape.16
  15.3 0.2 %convolution_convert_fusion = bf16[2,64,64]{2,1,0:T(8,128)(2,1)S(1)} fusion(f32[2,128,64]{1,0,2:T(2,128)S(1)} %get-tuple-element.6, f32[2,128,64]{1,0,2:T(2,128)S(1)} %get-tuple-element.5), kind=kOutput, calls=%fused_computation.2 | convolution fusion | flops 12591104 | bytes 147456 | tf_op jit(solution)/shard_map/sto,sti->soi/dot_general | solution.py:19
  15.5 0.1 convert_element_type.11
  15.6 0.1 collective-permute-start.2
  16.4 0.8 %collective-permute-done.4 = bf16[8,4096]{1,0:T(8,128)(2,1)S(1)} collective-permute-done((bf16[8,4096]{1,0:T(8,128)(2,1)S(1)}, bf16[8,4096]{1,0:T(8,128)(2,1)S(1)}, u32[]{:S(2)}, u32[]{:S(2)}) %collective-permute-start.4) | collective-permute-done | bytes 65568 | tf_op jit(solution)/shard_map/ppermute | solution.py:69
  17.2 0.0 collective-permute-done.2
  17.2 0.2 convolution_multiply_fusion
  17.4 1.5 %collective-permute-start.5 = (f32[4,16]{1,0:T(4,128)S(1)}, f32[4,16]{1,0:T(4,128)S(1)}, u32[]{:S(2)}, u32[]{:S(2)}) collective-permute-start(f32[4,16]{1,0:T(4,128)S(1)} %convolution_multiply_fusion), channel_id=1, source_target_pairs={{0,16},{16,0},{1,17},{17,1},{2,18},{18,2},{3,19},{19,3},{4,20},{20... | collective-permute-start | bytes 776 | tf_op jit(solution)/shard_map/ppermute | solution.py:69
  18.9 2.1 %collective-permute-done.5 = f32[4,16]{1,0:T(4,128)S(1)} collective-permute-done((f32[4,16]{1,0:T(4,128)S(1)}, f32[4,16]{1,0:T(4,128)S(1)}, u32[]{:S(2)}, u32[]{:S(2)}) %collective-permute-start.5) | collective-permute-done | bytes 288 | tf_op jit(solution)/shard_map/ppermute | solution.py:69
  21.0 0.7 %reshape.17 = f32[4,4,4]{2,1,0:T(4,128)} reshape(f32[4,16]{1,0:T(4,128)S(1)} %add.11) | data formatting | bytes 512 | tf_op jit(solution)/shard_map/reshape | solution.py:109
  (9 shorter events, 0.1 us)
Async XLA Ops:
  0.0 5.4 %copy-start = (bf16[1,512,2048]{2,1,0:T(8,128)(2,1)S(1)}, bf16[1,512,2048]{2,1,0:T(8,128)(2,1)}, u32[]{:S(2)}) copy-start(bf16[1,512,2048]{2,1,0:T(8,128)(2,1)} %param.7) | copy-start | bytes 6291460
  0.0 5.4 %copy-start.2 = (bf16[64,2048]{1,0:T(8,128)(2,1)S(1)}, bf16[64,2048]{1,0:T(8,128)(2,1)}, u32[]{:S(2)}) copy-start(bf16[64,2048]{1,0:T(8,128)(2,1)} %param.9) | copy-start | bytes 786436
  5.4 0.9 %copy-start.1 = (f32[64,512]{1,0:T(8,128)S(1)}, f32[64,512]{1,0:T(8,128)}, u32[]{:S(2)}) copy-start(f32[64,512]{1,0:T(8,128)} %shard_map.64) | copy-start | bytes 393220
  5.4 1.5 %copy-start.3 = (bf16[1,4,4096]{2,1,0:T(4,128)(2,1)S(1)}, bf16[1,4,4096]{2,1,0:T(4,128)(2,1)}, u32[]{:S(2)}) copy-start(bf16[1,4,4096]{2,1,0:T(4,128)(2,1)} %param.10) | copy-start | bytes 98308
  6.3 3.2 %collective-permute-start = (f32[256,128]{0,1:T(8,128)S(1)}, f32[256,128]{0,1:T(8,128)S(1)}, u32[]{:S(2)}, u32[]{:S(2)}) collective-permute-start(f32[256,128]{0,1:T(8,128)S(1)} %broadcast_select_fusion), channel_id=1, source_target_pairs={{0,1},{1,0},{2,3},{3,2},{4,5},{5,4},{6,7},{7,6},{8,9},{9,8},{10,11... | collective-permute-start | bytes 393224 | tf_op jit(solution)/shard_map/ppermute | solution.py:69
  6.9 4.6 %collective-permute-start.3 = (bf16[4,4096]{1,0:T(4,128)(2,1)S(1)}, bf16[4,4096]{1,0:T(4,128)(2,1)S(1)}, u32[]{:S(2)}, u32[]{:S(2)}) collective-permute-start(bf16[4,4096]{1,0:T(4,128)(2,1)S(1)} %bitcast.14), channel_id=1, source_target_pairs={{0,4},{4,0},{8,12},{12,8},{1,5},{5,1},{9,13},{13,9},{2,6},{6,2},{1... | collective-permute-start | bytes 98312 | tf_op jit(solution)/shard_map/ppermute | solution.py:69
  9.5 5.6 %collective-permute-start.1 = (f32[256,128]{0,1:T(8,128)S(1)}, f32[256,128]{0,1:T(8,128)S(1)}, u32[]{:S(2)}, u32[]{:S(2)}) collective-permute-start(f32[256,128]{0,1:T(8,128)S(1)} %select_add_fusion), channel_id=1, source_target_pairs={{0,2},{1,3},{2,0},{3,1},{4,6},{5,7},{6,4},{7,5},{8,10},{9,11},{10,... | collective-permute-start | bytes 393224 | tf_op jit(solution)/shard_map/ppermute | solution.py:69
  11.6 5.6 %collective-permute-start.4 = (bf16[8,4096]{1,0:T(8,128)(2,1)S(1)}, bf16[8,4096]{1,0:T(8,128)(2,1)S(1)}, u32[]{:S(2)}, u32[]{:S(2)}) collective-permute-start(bf16[8,4096]{1,0:T(8,128)(2,1)S(1)} %maximum_select_fusion.2), channel_id=1, source_target_pairs={{0,8},{4,12},{8,0},{12,4},{1,9},{5,13},{9,1},{13,5},{2,10},{6,14},... | collective-permute-start | bytes 196616 | tf_op jit(solution)/shard_map/ppermute | solution.py:69
  15.6 1.6 %collective-permute-start.2 = (bf16[2,4096]{1,0:T(2,128)(2,1)S(1)}, bf16[2,4096]{1,0:T(2,128)(2,1)S(1)}, u32[]{:S(2)}, u32[]{:S(2)}) collective-permute-start(bf16[2,4096]{1,0:T(2,128)(2,1)S(1)} %convert_element_type.11), channel_id=1, source_target_pairs={{0,1},{1,0},{2,3},{3,2},{4,5},{5,4},{6,7},{7,6},{8,9},{9,8},{10,11... | collective-permute-start | bytes 49160 | tf_op jit(solution)/shard_map/ppermute | solution.py:69
  17.4 3.6 %collective-permute-start.5 = (f32[4,16]{1,0:T(4,128)S(1)}, f32[4,16]{1,0:T(4,128)S(1)}, u32[]{:S(2)}, u32[]{:S(2)}) collective-permute-start(f32[4,16]{1,0:T(4,128)S(1)} %convolution_multiply_fusion), channel_id=1, source_target_pairs={{0,16},{16,0},{1,17},{17,1},{2,18},{18,2},{3,19},{19,3},{4,20},{20... | collective-permute-start | bytes 776 | tf_op jit(solution)/shard_map/ppermute | solution.py:69
